TPU v7x, 128 devices: a whole 4x4x4 slice. The times are simulated.
128 devices in a mesh: loop: 16 (over x_hi, z, core), width: 8 (over x_lo, y).
Axes of the slice: x: 4 (x_hi: 2, x_lo: 2; x = x_hi * 2 + x_lo), y: 4, z: 4, core: 2. Of those that a mesh axis runs over, the one named last changes fastest.
Arguments:
- queries: bfloat16 [16384, 4096], P('loop', 'width'), may hold values from -0.0625 to 0.0625
- passages: bfloat16 [16384, 4096], P('loop', 'width'), may hold values from -0.0625 to 0.0625
- teacher: bfloat16 [16384, 4096], P('loop'), may hold values from -5 to 12
- positives: int32 [16384], P('loop'), may hold values from 0 to 4095
Outputs:
- grad_queries: float32 [16384, 4096], P('loop', 'width')
- grad_passages: float32 [16384, 4096], P('loop', 'width')
All inputs are finite; a program needn't handle non-finite values.
Results may differ from a plain program's by a relative error of at most 0.0003.
Values may be sent and summed in bfloat16 or wider, within the bound.
No kernel may reach another device: no remote copies, remote signals or barrier semaphores. Data moves between devices by JAX's collectives and lax.ppermute only.
A program may use at most 192 MiB of HBM per device.

v0:
```python
import jax
import jax.numpy as jnp
from jax import lax
from jax.sharding import PartitionSpec as P

STEPS = 4
SCALE = 20.0


def shifted(block, axis, distance):
    devices = range(lax.axis_size(axis))
    route = [((i - distance) % len(devices), i) for i in devices]
    return lax.ppermute(block, axis, route)


def wide_dot(a, b):
    return jnp.dot(a, b, precision=lax.Precision.HIGH, preferred_element_type=jnp.float32)


def per_device(queries, passages, teacher, positives):
    rows = queries.shape[0]
    width = lax.axis_size("width")
    me = lax.axis_index("width")
    sub = rows // width
    window = STEPS * rows
    q_full = lax.all_gather(queries, "width", axis=1, tiled=True)
    p_cols = lax.all_to_all(passages, "width", 0, 1, tiled=True)
    held_cols = [p_cols]
    held = [passages]
    for step in range(1, STEPS):
        held_cols.append(shifted(held_cols[-1], "loop", 1))
        held.append(shifted(held[-1], "loop", 1))
    cols = jnp.concatenate(held_cols, 0)
    raw = jnp.einsum("qd,cd->qc", q_full, cols, preferred_element_type=jnp.float32)
    gathered = [
        lax.all_gather(raw[:, k * sub : (k + 1) * sub], "width", axis=1, tiled=True)
        for k in range(STEPS)
    ]
    scores = SCALE * raw
    index = positives[:, None]
    column = lax.broadcasted_iota(jnp.int32, teacher.shape, 1)
    t_pos = jnp.sum(jnp.where(column == index, teacher.astype(jnp.float32), 0.0), 1, keepdims=True)
    local = lax.broadcasted_iota(jnp.int32, (1, STEPS * sub), 1)
    wcol = local // sub * rows + me * sub + local % sub
    hit = wcol == index
    teach_cols = (
        lax.dynamic_slice_in_dim(teacher.reshape(rows, STEPS, width, sub), me, 1, 2)
        .reshape(rows, STEPS * sub)
        .astype(jnp.float32)
    )
    pos_part = jnp.sum(jnp.where(hit, scores, 0.0), 1)
    row_part = jnp.sum(scores, 1) - jnp.sum(teach_cols, 1)
    stats = lax.psum(jnp.stack([pos_part, row_part], 0), "width")
    s_pos = stats[0][:, None]
    total = window * (s_pos - t_pos) - stats[1][:, None]
    coef = SCALE * 2.0 / (window - 1)
    block_col = lax.broadcasted_iota(jnp.int32, (rows, rows), 1)
    query_wide = queries.astype(jnp.float32)
    grad_q = None
    terms = []
    for k in range(STEPS):
        block_scores = SCALE * gathered[k]
        errors = (
            s_pos
            - block_scores
            - (t_pos - teacher[:, k * rows : (k + 1) * rows].astype(jnp.float32))
        )
        block_hit = (block_col + k * rows == index).astype(jnp.float32)
        block_slopes = coef * (block_hit * total - errors)
        gq = wide_dot(block_slopes, held[k].astype(jnp.float32))
        grad_q = gq if grad_q is None else grad_q + gq
        terms.append(wide_dot(block_slopes.T, query_wide))
    grad_p = terms[STEPS - 1]
    for k in range(STEPS - 2, -1, -1):
        grad_p = shifted(grad_p, "loop", -1) + terms[k]
    return (grad_q, grad_p)


def solution(mesh):
    in_specs = (P("loop", "width"), P("loop", "width"), P("loop", None), P("loop"))
    out_specs = (P("loop", "width"), P("loop", "width"))
    return jax.shard_map(
        per_device, mesh=mesh, in_specs=in_specs, out_specs=out_specs, check_vma=False
    )
```

profile of v0, /device:TPU:0, one launch (start us, length us, event | category | flops | bytes accessed | tf_op | source)
XLA Modules:
  0.0 438.1 jit_solution(10185207552571837070)
XLA Ops:
  7.2 0.0 copy-start.6
  7.2 0.0 all-gather.6.cloned.1.call-start
  7.2 0.7 all-gather.6.cloned.1.call-update
  7.9 0.0 all-gather.14.cloned.1.call-start
  8.0 26.1 %all_to_all.19 = bf16[8,128,512]{2,1,0:T(8,128)(2,1)S(1)} all-to-all(bf16[8,128,512]{2,1,0:T(8,128)(2,1)} %bitcast.24), channel_id=1, replica_groups=mesh['loop'=16,'width'=8] {'width'}, dimensions={0} | all-to-all | bytes 2097152 | tf_op jit(solution)/shard_map/all_to_all | solution.py:27
  34.1 0.7 copy.14
  34.7 0.1 collective-permute-start
  34.8 40.4 %collective-permute-done = bf16[128,4096]{0,1:T(8,128)(2,1)S(1)} collective-permute-done((bf16[128,4096]{0,1:T(8,128)(2,1)S(1)}, bf16[128,4096]{0,1:T(8,128)(2,1)S(1)}, u32[]{:S(2)}, u32[]{:S(2)}) %collective-permute-start) | collective-permute-done | bytes 1048608 | tf_op jit(solution)/shard_map/ppermute | solution.py:13
  75.2 0.0 collective-permute-start.1
  75.2 40.4 %collective-permute-done.1 = bf16[128,4096]{0,1:T(8,128)(2,1)S(1)} collective-permute-done((bf16[128,4096]{0,1:T(8,128)(2,1)S(1)}, bf16[128,4096]{0,1:T(8,128)(2,1)S(1)}, u32[]{:S(2)}, u32[]{:S(2)}) %collective-permute-start.1) | collective-permute-done | bytes 1048608 | tf_op jit(solution)/shard_map/ppermute | solution.py:13
  115.7 0.0 collective-permute-start.2
  115.7 28.3 %collective-permute-done.2 = bf16[128,4096]{0,1:T(8,128)(2,1)} collective-permute-done((bf16[128,4096]{0,1:T(8,128)(2,1)S(1)}, bf16[128,4096]{0,1:T(8,128)(2,1)}, u32[]{:S(2)}, u32[]{:S(2)}) %collective-permute-start.2) | collective-permute-done | bytes 1048608 | tf_op jit(solution)/shard_map/ppermute | solution.py:13
  144.0 0.0 copy-done.6
  144.0 8.5 %select_reduce_fusion.1 = (f32[1024]{0:T(1024)S(1)}, f32[1024]{0:T(1024)S(1)}, f32[1024,512]{0,1:T(8,128)S(1)}) fusion(s32[1024]{0:T(1024)S(1)} %copy-done.6, s32[512]{0:T(512)S(1)} %fusion.23, bf16[1024,4096]{1,0:T(8,128)(2,1)} %all-gather.6.cloned.1.call-done, bf16[128,4096]{0,1:T(8,128)(2,1)} %collective-permute-done.2, ...), kind=kOutput, calls=%fused_computation.17 | convolution fusion | flops 4314363904 | bytes 14694400 | tf_op jit(solution)/shard_map/qd,cd->qc/dot_general | solution.py:34
  152.5 1.4 fusion.53
  153.9 0.0 all-gather.14.cloned.1.call-update
  153.9 0.0 all-gather.12.cloned.1.call-start
  153.9 0.7 all-gather.12.cloned.1.call-update
  154.6 0.0 all-gather.8.cloned.1.call-start
  154.7 0.5 all-gather.8.cloned.1.call-update
  155.2 0.3 all-gather.10.cloned.1.call-start
  155.5 0.2 all-gather.10.cloned.1.call-update
  155.8 9.5 %copy.23 = bf16[128,8,32,128]{3,2,1,0:T(8,128)(2,1)} copy(bf16[128,8,32,128]{3,1,2,0:T(8,128)(2,1)} %bitcast.21) | data formatting | bytes 16777216
  165.3 5.9 %fusion.52 = (bf16[1024,1024]{1,0:T(8,128)(2,1)}, bf16[1024,1024]{1,0:T(8,128)(2,1)}, bf16[1024,1024]{1,0:T(8,128)(2,1)}, bf16[1024,1024]{1,0:T(8,128)(2,1)S(1)}) fusion(bf16[1024,4096]{1,0:T(8,128)(2,1)} %param.6), kind=kLoop, calls=%fused_computation.71 | loop fusion | bytes 16777216 | tf_op jit(solution)/shard_map/slice | solution.py:66
  171.2 4.0 copy.22
  175.1 7.6 %convert_reduce_fusion = f32[1024]{0:T(1024)S(1)} fusion(bf16[1024,4,8,128]{3,2,1,0:T(8,128)(2,1)} %bitcast.22, s32[]{:T(128)S(6)} %select_n.36), kind=kLoop, calls=%fused_computation.16 | loop fusion | flops 1047552 | bytes 1052676 | tf_op jit(solution)/shard_map/reduce_sum | solution.py:52
  182.8 0.0 copy-start.3
  182.8 6.4 %select_reduce_fusion = f32[1024]{0:T(1024)S(1)} fusion(bf16[1024,4096]{1,0:T(8,128)(2,1)} %param.6, s32[1024]{0:T(1024)S(1)} %copy-done.6), kind=kLoop, calls=%fused_computation | loop fusion | flops 16776192 | bytes 8396800 | tf_op jit(solution)/shard_map/reduce_sum | solution.py:42
  189.2 20.3 %psum.7 = f32[2,1024]{1,0:T(2,128)S(1)} all-reduce(f32[2,1024]{1,0:T(2,128)S(1)} %pad_maximum_fusion), channel_id=1, replica_groups=mesh['loop'=16,'width'=8] {'width'}, use_global_device_ids=true, to_apply=%region_3.4 | all-reduce | flops 2048 | bytes 16384 | tf_op jit(solution)/shard_map/psum | solution.py:53
  209.6 0.0 all-gather.14.cloned.1.call-done
  209.6 0.0 copy-done.3
  209.6 0.0 copy-start.4
  209.6 7.1 %fusion.16 = f32[1024,512]{1,0:T(8,128)} fusion(bf16[1024,512]{1,0:T(8,128)(2,1)S(1)} %copy-done.3, bf16[1024,1024]{0,1:T(8,128)(2,1)} %copy.22, f32[1024,1024]{0,1:T(8,128)} %all-gather.14.cloned.1.call-done, f32[1024]{0:T(1024)S(1)} %select_reduce_fusion, f32[1024]{0:T(1024)S(1)} %bitcast.29, f32[1024]{0:T(1024)S(1)} %multiply_subtract_fusion, ...), kind=kOutput, calls=%fused_computation.26 | convolution fusion | flops 3230662656 | bytes 9457664 | tf_op jit(solution)/shard_map/dot_general | solution.py:17
  216.7 0.5 collective-permute-start.6
  217.2 0.0 copy-done.4
  217.2 0.5 collective-permute-start.3
  217.7 39.7 %collective-permute-done.3 = bf16[1024,512]{1,0:T(8,128)(2,1)} collective-permute-done((bf16[1024,512]{1,0:T(8,128)(2,1)S(1)}, bf16[1024,512]{1,0:T(8,128)(2,1)}, u32[]{:S(2)}, u32[]{:S(2)}) %collective-permute-start.3) | collective-permute-done | bytes 1048608 | tf_op jit(solution)/shard_map/ppermute | solution.py:13
  257.4 0.0 collective-permute-start.4
  257.4 3.9 copy.21
  261.3 3.9 copy.20
  265.3 2.5 copy.19
  267.8 8.7 %all-gather.12.cloned.1.call-done = f32[1024,1024]{0,1:T(8,128)} async-done(((f32[1024,128]{0,1:T(8,128)}), f32[1024,1024]{0,1:T(8,128)}) %all-gather.12.cloned.1.call-update) | async-done | bytes 4194320 | tf_op jit(solution)/shard_map/all_gather | solution.py:36
  276.5 0.0 collective-permute-done.6
  276.5 7.6 %convolution_add_fusion = f32[1024,512]{1,0:T(8,128)} fusion(f32[1024,512]{1,0:T(8,128)} %collective-permute-done.6, bf16[1024,512]{1,0:T(8,128)(2,1)S(1)} %copy-done.3, bf16[1024,1024]{0,1:T(8,128)(2,1)} %copy.21, f32[1024,1024]{0,1:T(8,128)} %all-gather.12.cloned.1.call-done, f32[1024]{0:T(1024)S(1)} %select_reduce_fusion, f32[1024]{0:T(1024)S(1)} %bitcast.30, ...), kind=kOutput, calls=%fused_computation.20 | convolution fusion | flops 3231186944 | bytes 11554816 | tf_op jit(solution)/shard_map/dot_general | solution.py:17
  284.1 4.0 collective-permute-start.7
  288.1 0.0 collective-permute-done.4
  288.1 0.2 collective-permute-start.5
  288.3 55.0 %all-gather.8.cloned.1.call-done = f32[1024,1024]{0,1:T(8,128)} async-done(((f32[1024,128]{0,1:T(8,128)}), f32[1024,1024]{0,1:T(8,128)}) %all-gather.8.cloned.1.call-update) | async-done | bytes 4194320 | tf_op jit(solution)/shard_map/all_gather | solution.py:36
  343.3 5.8 %fusion.11 = f32[1024,512]{1,0:T(8,128)S(1)} fusion(bf16[1024,512]{1,0:T(8,128)(2,1)S(1)} %copy-done.3, bf16[1024,1024]{0,1:T(8,128)(2,1)} %copy.19, f32[1024,1024]{0,1:T(8,128)} %all-gather.8.cloned.1.call-done, f32[1024]{0:T(1024)S(1)} %select_reduce_fusion, f32[1024]{0:T(1024)S(1)} %bitcast.31, f32[1024]{0:T(1024)S(1)} %multiply_subtract_fusion, ...), kind=kOutput, calls=%fused_computation.21 | convolution fusion | flops 3230662656 | bytes 9453568 | tf_op jit(solution)/shard_map/dot_general | solution.py:17
  349.1 6.3 %fusion.15 = f32[1024,512]{1,0:T(8,128)} fusion(bf16[1024,512]{1,0:T(8,128)(2,1)} %collective-permute-done.4, bf16[1024,1024]{0,1:T(8,128)(2,1)} %copy.21, f32[1024,1024]{0,1:T(8,128)S(1)} %copy-done.10, f32[1024]{0:T(1024)S(1)} %select_reduce_fusion, f32[1024]{0:T(1024)S(1)} %bitcast.32, f32[1024]{0:T(1024)S(1)} %multiply_subtract_fusion, ...), kind=kOutput, calls=%fused_computation.25 | convolution fusion | flops 3230662656 | bytes 9457664 | tf_op jit(solution)/shard_map/dot_general | solution.py:17
  355.4 38.5 %all-gather.10.cloned.1.call-done = f32[1024,1024]{0,1:T(8,128)} async-done(((f32[1024,128]{0,1:T(8,128)}), f32[1024,1024]{0,1:T(8,128)}) %all-gather.10.cloned.1.call-update) | async-done | bytes 4194320 | tf_op jit(solution)/shard_map/all_gather | solution.py:36
  393.9 5.1 %fusion.13 = f32[1024,512]{1,0:T(8,128)S(1)} fusion(bf16[1024,512]{1,0:T(8,128)(2,1)S(1)} %copy-done.3, bf16[1024,1024]{0,1:T(8,128)(2,1)} %copy.20, f32[1024,1024]{0,1:T(8,128)} %all-gather.10.cloned.1.call-done, f32[1024]{0:T(1024)S(1)} %select_reduce_fusion, f32[1024]{0:T(1024)S(1)} %bitcast.33, f32[1024]{0:T(1024)S(1)} %multiply_subtract_fusion, ...), kind=kOutput, calls=%fused_computation.23 | convolution fusion | flops 3230662656 | bytes 9457664 | tf_op jit(solution)/shard_map/dot_general | solution.py:17
  399.1 0.0 copy-start.2
  399.1 0.0 copy-start.5
  399.1 0.0 collective-permute-done.7
  399.1 2.2 add.95
  401.3 4.6 %collective-permute-start.8 = (f32[1024,512]{1,0:T(8,128)S(1)}, f32[1024,512]{1,0:T(8,128)S(1)}, u32[]{:S(2)}, u32[]{:S(2)}) collective-permute-start(f32[1024,512]{1,0:T(8,128)S(1)} %add.95), channel_id=1, source_target_pairs={{8,0},{16,8},{24,16},{32,24},{40,32},{48,40},{56,48},{64,56},{72,6... | collective-permute-start | bytes 6291464 | tf_op jit(solution)/shard_map/ppermute | solution.py:13
  406.0 3.0 fusion.12
  409.0 0.0 copy-start.11
  409.0 4.4 fusion.14
  413.4 0.0 collective-permute-done.5
  413.4 5.8 %add_add_fusion = f32[1024,512]{1,0:T(8,128)} fusion(f32[1024,512]{1,0:T(8,128)S(1)} %copy-done.11, f32[1024,512]{1,0:T(8,128)S(1)} %fusion.12, f32[1024,512]{1,0:T(8,128)S(1)} %fusion.14, bf16[1024,512]{1,0:T(8,128)(2,1)} %collective-permute-done.5, bf16[1024,1024]{0,1:T(8,128)(2,1)S(1)} %copy-done, f32[1024,1024]{0,1:T(8,128)S(1)} %copy-done.7, ...), kind=kOutput, calls=%fused_computation.15 | convolution fusion | flops 3232235520 | bytes 15749120 | tf_op jit(solution)/shard_map/dot_general | solution.py:17
  419.2 10.3 %collective-permute-done.8 = f32[1024,512]{1,0:T(8,128)S(1)} collective-permute-done((f32[1024,512]{1,0:T(8,128)S(1)}, f32[1024,512]{1,0:T(8,128)S(1)}, u32[]{:S(2)}, u32[]{:S(2)}) %collective-permute-start.8) | collective-permute-done | bytes 2097184 | tf_op jit(solution)/shard_map/ppermute | solution.py:13
  429.5 1.8 add.96
  (24 shorter events, 0.1 us)
Async XLA Ops:
  7.2 136.8 %copy-start.6 = (s32[1024]{0:T(1024)S(1)}, s32[1024]{0:T(1024)}, u32[]{:S(2)}) copy-start(s32[1024]{0:T(1024)} %param.7) | copy-start | bytes 12292
  7.2 136.8 %all-gather.6.cloned.1.call-start = ((), (), s32[]{:S(2)}) async-start(), calls=%async_computation.1 | async-start | bytes 9437184 | tf_op jit(solution)/shard_map/all_gather | solution.py:26
  7.9 201.7 %all-gather.14.cloned.1.call-start = ((), (), s32[]{:S(2)}) async-start(), calls=%async_computation.5 | async-start | bytes 4718592 | tf_op jit(solution)/shard_map/all_gather | solution.py:36
  34.7 40.5 %collective-permute-start = (bf16[128,4096]{0,1:T(8,128)(2,1)S(1)}, bf16[128,4096]{0,1:T(8,128)(2,1)S(1)}, u32[]{:S(2)}, u32[]{:S(2)}) collective-permute-start(bf16[128,4096]{0,1:T(8,128)(2,1)S(1)} %bitcast.25), channel_id=1, source_target_pairs={{120,0},{0,8},{8,16},{16,24},{24,32},{32,40},{40,48},{48,56},{56,6... | collective-permute-start | bytes 3145736 | tf_op jit(solution)/shard_map/ppermute | solution.py:13
  75.2 40.4 %collective-permute-start.1 = (bf16[128,4096]{0,1:T(8,128)(2,1)S(1)}, bf16[128,4096]{0,1:T(8,128)(2,1)S(1)}, u32[]{:S(2)}, u32[]{:S(2)}) collective-permute-start(bf16[128,4096]{0,1:T(8,128)(2,1)S(1)} %collective-permute-done), channel_id=1, source_target_pairs={{120,0},{0,8},{8,16},{16,24},{24,32},{32,40},{40,48},{48,56},{56,6... | collective-permute-start | bytes 3145736 | tf_op jit(solution)/shard_map/ppermute | solution.py:13
  115.7 28.3 %collective-permute-start.2 = (bf16[128,4096]{0,1:T(8,128)(2,1)S(1)}, bf16[128,4096]{0,1:T(8,128)(2,1)}, u32[]{:S(2)}, u32[]{:S(2)}) collective-permute-start(bf16[128,4096]{0,1:T(8,128)(2,1)S(1)} %collective-permute-done.1), channel_id=1, source_target_pairs={{120,0},{0,8},{8,16},{16,24},{24,32},{32,40},{40,48},{48,56},{56,6... | collective-permute-start | bytes 3145736 | tf_op jit(solution)/shard_map/ppermute | solution.py:13
  153.9 122.6 %all-gather.12.cloned.1.call-start = ((), (), s32[]{:S(2)}) async-start(), calls=%async_computation.4 | async-start | bytes 4718592 | tf_op jit(solution)/shard_map/all_gather | solution.py:36
  154.6 188.6 %all-gather.8.cloned.1.call-start = ((), (), s32[]{:S(2)}) async-start(), calls=%async_computation.2 | async-start | bytes 4718592 | tf_op jit(solution)/shard_map/all_gather | solution.py:36
  155.2 238.7 %all-gather.10.cloned.1.call-start = ((), (), s32[]{:S(2)}) async-start(), calls=%async_computation.3 | async-start | bytes 4718592 | tf_op jit(solution)/shard_map/all_gather | solution.py:36
  182.8 26.8 %copy-start.3 = (bf16[1024,512]{1,0:T(8,128)(2,1)S(1)}, bf16[1024,512]{1,0:T(8,128)(2,1)}, u32[]{:S(2)}) copy-start(bf16[1024,512]{1,0:T(8,128)(2,1)} %param.4) | copy-start | bytes 3145732
  209.6 7.6 %copy-start.4 = (bf16[1024,512]{1,0:T(8,128)(2,1)S(1)}, bf16[1024,512]{1,0:T(8,128)(2,1)}, u32[]{:S(2)}) copy-start(bf16[1024,512]{1,0:T(8,128)(2,1)} %param.5) | copy-start | bytes 3145732
  216.7 59.8 %collective-permute-start.6 = (f32[1024,512]{1,0:T(8,128)}, f32[1024,512]{1,0:T(8,128)}, u32[]{:S(2)}, u32[]{:S(2)}) collective-permute-start(f32[1024,512]{1,0:T(8,128)} %fusion.16), channel_id=1, source_target_pairs={{8,0},{16,8},{24,16},{32,24},{40,32},{48,40},{56,48},{64,56},{72,6... | collective-permute-start | bytes 6291464 | tf_op jit(solution)/shard_map/ppermute | solution.py:13
  217.2 40.2 %collective-permute-start.3 = (bf16[1024,512]{1,0:T(8,128)(2,1)S(1)}, bf16[1024,512]{1,0:T(8,128)(2,1)}, u32[]{:S(2)}, u32[]{:S(2)}) collective-permute-start(bf16[1024,512]{1,0:T(8,128)(2,1)S(1)} %copy-done.4), channel_id=1, source_target_pairs={{120,0},{0,8},{8,16},{16,24},{24,32},{32,40},{40,48},{48,56},{56,6... | collective-permute-start | bytes 3145736 | tf_op jit(solution)/shard_map/ppermute | solution.py:13
  257.4 30.7 %collective-permute-start.4 = (bf16[1024,512]{1,0:T(8,128)(2,1)}, bf16[1024,512]{1,0:T(8,128)(2,1)}, u32[]{:S(2)}, u32[]{:S(2)}) collective-permute-start(bf16[1024,512]{1,0:T(8,128)(2,1)} %collective-permute-done.3), channel_id=1, source_target_pairs={{120,0},{0,8},{8,16},{16,24},{24,32},{32,40},{40,48},{48,56},{56,6... | collective-permute-start | bytes 3145736 | tf_op jit(solution)/shard_map/ppermute | solution.py:13
  284.1 115.0 %collective-permute-start.7 = (f32[1024,512]{1,0:T(8,128)}, f32[1024,512]{1,0:T(8,128)}, u32[]{:S(2)}, u32[]{:S(2)}) collective-permute-start(f32[1024,512]{1,0:T(8,128)} %convolution_add_fusion), channel_id=1, source_target_pairs={{8,0},{16,8},{24,16},{32,24},{40,32},{48,40},{56,48},{64,56},{72,6... | collective-permute-start | bytes 6291464 | tf_op jit(solution)/shard_map/ppermute | solution.py:13
  288.1 125.2 %collective-permute-start.5 = (bf16[1024,512]{1,0:T(8,128)(2,1)}, bf16[1024,512]{1,0:T(8,128)(2,1)}, u32[]{:S(2)}, u32[]{:S(2)}) collective-permute-start(bf16[1024,512]{1,0:T(8,128)(2,1)} %collective-permute-done.4), channel_id=1, source_target_pairs={{120,0},{0,8},{8,16},{16,24},{24,32},{32,40},{40,48},{48,56},{56,6... | collective-permute-start | bytes 3145736 | tf_op jit(solution)/shard_map/ppermute | solution.py:13
  343.3 5.8 %copy-start.10 = (f32[1024,1024]{0,1:T(8,128)S(1)}, f32[1024,1024]{0,1:T(8,128)}, u32[]{:S(2)}) copy-start(f32[1024,1024]{0,1:T(8,128)} %all-gather.12.cloned.1.call-done) | copy-start | bytes 12582916
  393.9 12.1 %copy-start.8 = (f32[1024,1024]{0,1:T(8,128)S(1)}, f32[1024,1024]{0,1:T(8,128)}, u32[]{:S(2)}) copy-start(f32[1024,1024]{0,1:T(8,128)} %all-gather.8.cloned.1.call-done) | copy-start | bytes 12582916
  399.1 6.9 %copy-start.2 = (bf16[1024,1024]{0,1:T(8,128)(2,1)S(1)}, bf16[1024,1024]{0,1:T(8,128)(2,1)}, u32[]{:S(2)}) copy-start(bf16[1024,1024]{0,1:T(8,128)(2,1)} %copy.19) | copy-start | bytes 6291460
  399.1 6.9 %copy-start.5 = (bf16[1024,512]{1,0:T(8,128)(2,1)S(1)}, bf16[1024,512]{1,0:T(8,128)(2,1)}, u32[]{:S(2)}) copy-start(bf16[1024,512]{1,0:T(8,128)(2,1)} %param.5) | copy-start | bytes 3145732
  401.3 7.6 %copy-start.1 = (bf16[1024,1024]{0,1:T(8,128)(2,1)S(1)}, bf16[1024,1024]{0,1:T(8,128)(2,1)}, u32[]{:S(2)}) copy-start(bf16[1024,1024]{0,1:T(8,128)(2,1)} %copy.20) | copy-start | bytes 6291460
  401.3 7.6 %copy-start.9 = (f32[1024,1024]{0,1:T(8,128)S(1)}, f32[1024,1024]{0,1:T(8,128)}, u32[]{:S(2)}) copy-start(f32[1024,1024]{0,1:T(8,128)} %all-gather.10.cloned.1.call-done) | copy-start | bytes 12582916
  401.3 28.2 %collective-permute-start.8 = (f32[1024,512]{1,0:T(8,128)S(1)}, f32[1024,512]{1,0:T(8,128)S(1)}, u32[]{:S(2)}, u32[]{:S(2)}) collective-permute-start(f32[1024,512]{1,0:T(8,128)S(1)} %add.95), channel_id=1, source_target_pairs={{8,0},{16,8},{24,16},{32,24},{40,32},{48,40},{56,48},{64,56},{72,6... | collective-permute-start | bytes 6291464 | tf_op jit(solution)/shard_map/ppermute | solution.py:13
  409.0 4.4 %copy-start = (bf16[1024,1024]{0,1:T(8,128)(2,1)S(1)}, bf16[1024,1024]{0,1:T(8,128)(2,1)}, u32[]{:S(2)}) copy-start(bf16[1024,1024]{0,1:T(8,128)(2,1)} %copy.22) | copy-start | bytes 6291460
  409.0 4.4 %copy-start.7 = (f32[1024,1024]{0,1:T(8,128)S(1)}, f32[1024,1024]{0,1:T(8,128)}, u32[]{:S(2)}) copy-start(f32[1024,1024]{0,1:T(8,128)} %all-gather.14.cloned.1.call-done) | copy-start | bytes 12582916
  409.0 4.4 %copy-start.11 = (f32[1024,512]{1,0:T(8,128)S(1)}, f32[1024,512]{1,0:T(8,128)}, u32[]{:S(2)}) copy-start(f32[1024,512]{1,0:T(8,128)} %fusion.15) | copy-start | bytes 6291460
Sparse Core Ops, SparseCore 0:
  9.6 98.8 all-gather.5
  154.0 50.4 all-gather.13
  206.2 70.2 all-gather.11
  278.0 65.2 all-gather.7
  344.7 49.1 all-gather.9
where the time goes:
time: 444 us; the launch traced here: 438 us
  waiting for transfers between devices  263 us (59%)
  matrix products  53.6 us (12%)
  blocking collectives  46.4 us (10%)
  local copies, waits for them, and re-layouts  31.8 us (7%)
  other arithmetic  18.1 us (4%)
  between operations  14.3 us (3%)
  starting transfers between devices  10.4 us (2%)
    ppermute x9, waiting for transfers between devices, shifted(): return lax.ppermute(block, axis, route)  159 us
    all_gather x4, waiting for transfers between devices, per_device(): lax.all_gather(raw[:, k * sub:(k + 1) * sub], 'width', axis=1, tiled=True)  102 us
    dot_general x8, matrix products, wide_dot(): jnp.dot(a, b, precision=lax.Precision.HIGH, preferred_element_type=jnp.fl...  45.1 us
    all_to_all x1, blocking collectives, per_device(): p_cols = lax.all_to_all(passages, 'width', 0, 1, tiled=True)  26.1 us
    unnamed x29, local copies, waits for them, and re-layouts  23.9 us
    psum x1, blocking collectives, per_device(): stats = lax.psum(jnp.stack([pos_part, row_part], 0), 'width')  20.3 us
    ppermute x9, starting transfers between devices, shifted(): return lax.ppermute(block, axis, route)  9.88 us
  transfers between devices with their start and end apart: 14, of which 8 were waited for; matrix products, arithmetic and copies ran while one was open for 21% of the time, Pallas kernels for 0%

commit v1 on v0

--- a/solution.py
+++ b/solution.py
@@ -32,10 +32,20 @@
         held.append(shifted(held[-1], "loop", 1))
     cols = jnp.concatenate(held_cols, 0)
     raw = jnp.einsum("qd,cd->qc", q_full, cols, preferred_element_type=jnp.float32)
-    gathered = [
-        lax.all_gather(raw[:, k * sub : (k + 1) * sub], "width", axis=1, tiled=True)
-        for k in range(STEPS)
-    ]
+
+    def link_squares(mine_x, axis_tag):
+        all_values = jnp.concatenate(
+            lax.all_to_all(
+                jnp.stack(lax.axis_size(axis_tag) * [mine_x], 0),
+                concat_axis=0,
+                split_axis=0,
+                axis_name=axis_tag,
+            ),
+            1,
+        )
+        return all_values
+
+    gathered = [link_squares(raw[:, k * sub : (k + 1) * sub], "width") for k in range(STEPS)]
     scores = SCALE * raw
     index = positives[:, None]
     column = lax.broadcasted_iota(jnp.int32, teacher.shape, 1)

time: 444 us -> 545 us (1.23)
  waiting for transfers between devices: 263 us -> 312 us
  local copies, waits for them, and re-layouts: 31.8 us -> 63.4 us
  matrix products: 53.6 us -> 29.1 us
  other arithmetic: 18.1 us -> 39.9 us
  starting transfers between devices: 10.4 us -> 31.3 us
    all_to_all x0 -> x4, waiting for transfers between devices: none -> 147 us  [link_squares(): lax.all_to_all(jnp.stack(lax.axis_size(axis_tag) * [mine_x], 0), concat_a...]
    all_gather x4 -> x0, waiting for transfers between devices: 102 us -> none  [per_device(): lax.all_gather(raw[:, k * sub:(k + 1) * sub], 'width', axis=1, tiled=True)]
    dot_general x8, matrix products: 45.1 us -> 20.3 us  [wide_dot(): jnp.dot(a, b, precision=lax.Precision.HIGH, preferred_element_type=jnp.fl...]
    mul x0 -> x5, other arithmetic: none -> 23.8 us  [the longest x4 15.3 us: per_device(): block_scores = SCALE * gathered[k]]
    all_to_all x0 -> x4, local copies, waits for them, and re-layouts: none -> 21.5 us  [link_squares(): lax.all_to_all(jnp.stack(lax.axis_size(axis_tag) * [mine_x], 0), concat_a...]
    all_to_all x0 -> x4, starting transfers between devices: none -> 19.2 us  [link_squares(): lax.all_to_all(jnp.stack(lax.axis_size(axis_tag) * [mine_x], 0), concat_a...]
    another operation x0 -> x4, local copies, waits for them, and re-layouts: none -> 8.89 us  [link_squares(): jnp.stack(lax.axis_size(axis_tag) * [mine_x], 0)]
    unnamed x29 -> x19, local copies, waits for them, and re-layouts: 23.9 us -> 25.7 us
  transfers between devices with their start and end apart: 14 -> 14, of which waited for: 8 -> 10; matrix products, arithmetic and copies ran while one was open for 21% -> 17% of each run, Pallas kernels for 0% -> 0%
where the time goes in v1:
time: 545 us; the launch traced here: 537 us
  waiting for transfers between devices  312 us (57%)
  local copies, waits for them, and re-layouts  63.4 us (12%)
  blocking collectives  46.5 us (9%)
  other arithmetic  39.9 us (7%)
  starting transfers between devices  31.3 us (6%)
  matrix products  29.1 us (5%)
  between operations  14.5 us (3%)
    ppermute x9, waiting for transfers between devices, shifted(): return lax.ppermute(block, axis, route)  164 us
    all_to_all x4, waiting for transfers between devices, link_squares(): lax.all_to_all(jnp.stack(lax.axis_size(axis_tag) * [mine_x], 0), concat_a...  147 us
    all_to_all x1, blocking collectives, per_device(): p_cols = lax.all_to_all(passages, 'width', 0, 1, tiled=True)  26.1 us
    unnamed x19, local copies, waits for them, and re-layouts  25.7 us
    all_to_all x4, local copies, waits for them, and re-layouts, link_squares(): lax.all_to_all(jnp.stack(lax.axis_size(axis_tag) * [mine_x], 0), concat_a...  21.5 us
    psum x1, blocking collectives, per_device(): stats = lax.psum(jnp.stack([pos_part, row_part], 0), 'width')  20.5 us
    dot_general x8, matrix products, wide_dot(): jnp.dot(a, b, precision=lax.Precision.HIGH, preferred_element_type=jnp.fl...  20.3 us
    all_to_all x4, starting transfers between devices, link_squares(): lax.all_to_all(jnp.stack(lax.axis_size(axis_tag) * [mine_x], 0), concat_a...  19.2 us
  transfers between devices with their start and end apart: 14, of which 10 were waited for; matrix products, arithmetic and copies ran while one was open for 17% of the time, Pallas kernels for 0%

profile of v1, /device:TPU:0, one launch (start us, length us, event | category | flops | bytes accessed | tf_op | source)
XLA Modules:
  0.0 536.5 jit_solution(486693796917809921)
XLA Ops:
  7.2 0.0 all-gather.2.cloned.1.call-start
  7.2 0.7 all-gather.2.cloned.1.call-update
  7.9 26.1 %all_to_all.39 = bf16[8,128,512]{2,1,0:T(8,128)(2,1)S(1)} all-to-all(bf16[8,128,512]{2,1,0:T(8,128)(2,1)} %bitcast.72), channel_id=1, replica_groups=mesh['loop'=16,'width'=8] {'width'}, dimensions={0} | all-to-all | bytes 2097152 | tf_op jit(solution)/shard_map/all_to_all | solution.py:27
  34.0 0.7 copy.24
  34.6 0.1 collective-permute-start
  34.7 40.4 %collective-permute-done = bf16[128,4096]{0,1:T(8,128)(2,1)S(1)} collective-permute-done((bf16[128,4096]{0,1:T(8,128)(2,1)S(1)}, bf16[128,4096]{0,1:T(8,128)(2,1)S(1)}, u32[]{:S(2)}, u32[]{:S(2)}) %collective-permute-start) | collective-permute-done | bytes 1048608 | tf_op jit(solution)/shard_map/ppermute | solution.py:13
  75.1 40.5 %collective-permute-done.1 = bf16[128,4096]{0,1:T(8,128)(2,1)} collective-permute-done((bf16[128,4096]{0,1:T(8,128)(2,1)S(1)}, bf16[128,4096]{0,1:T(8,128)(2,1)}, u32[]{:S(2)}, u32[]{:S(2)}) %collective-permute-start.1) | collective-permute-done | bytes 1048608 | tf_op jit(solution)/shard_map/ppermute | solution.py:13
  115.7 28.3 %collective-permute-done.2 = bf16[128,4096]{0,1:T(8,128)(2,1)} collective-permute-done((bf16[128,4096]{0,1:T(8,128)(2,1)}, bf16[128,4096]{0,1:T(8,128)(2,1)}, u32[]{:S(2)}, u32[]{:S(2)}) %collective-permute-start.2) | collective-permute-done | bytes 1048608 | tf_op jit(solution)/shard_map/ppermute | solution.py:13
  143.9 8.8 %select_reduce_fusion.1 = (f32[1024]{0:T(1024)S(1)}, f32[1024]{0:T(1024)S(1)}, f32[1024,512]{0,1:T(8,128)S(1)}) fusion(s32[1024]{0:T(1024)S(1)} %copy-done.6, s32[512]{0:T(512)S(1)} %fusion.29, bf16[1024,4096]{1,0:T(8,128)(2,1)} %all-gather.2.cloned.1.call-done, bf16[128,4096]{0,1:T(8,128)(2,1)} %collective-permute-done.2, ...), kind=kOutput, calls=%fused_computation.33 | convolution fusion | flops 4314363904 | bytes 14694400 | tf_op jit(solution)/shard_map/qd,cd->qc/dot_general | solution.py:34
  152.7 0.1 fusion.35
  152.9 0.2 copy.34
  153.1 2.2 stack.17
  155.3 5.0 all-to-all-start.4
  160.3 0.2 copy.31
  160.5 49.1 %all-to-all-done.4 = f32[8,1024,128]{2,1,0:T(8,128)} async-done(((f32[8,1024,128]{2,1,0:T(8,128)}), f32[8,1024,128]{2,1,0:T(8,128)}, u32[]{:S(2)}, u32[]{:S(2)}) %all-to-all-start.4) | async-done | bytes 4194336 | tf_op jit(solution)/shard_map/all_to_all | solution.py:38
  209.6 2.2 stack.16
  211.8 4.6 all-to-all-start.3
  216.4 0.2 copy.28
  216.6 49.3 %all-to-all-done.3 = f32[8,1024,128]{2,1,0:T(8,128)} async-done(((f32[8,1024,128]{2,1,0:T(8,128)}), f32[8,1024,128]{2,1,0:T(8,128)}, u32[]{:S(2)}, u32[]{:S(2)}) %all-to-all-start.3) | async-done | bytes 4194336 | tf_op jit(solution)/shard_map/all_to_all | solution.py:38
  265.9 2.2 stack.15
  268.1 4.6 all-to-all-start.2
  272.7 0.2 copy.25
  272.9 48.9 %all-to-all-done.2 = f32[8,1024,128]{2,1,0:T(8,128)} async-done(((f32[8,1024,128]{2,1,0:T(8,128)}), f32[8,1024,128]{2,1,0:T(8,128)}, u32[]{:S(2)}, u32[]{:S(2)}) %all-to-all-start.2) | async-done | bytes 4194336 | tf_op jit(solution)/shard_map/all_to_all | solution.py:38
  321.9 2.2 stack.14
  324.1 5.1 all-to-all-start.1
  329.1 9.5 %copy.41 = bf16[128,8,32,128]{3,2,1,0:T(8,128)(2,1)} copy(bf16[128,8,32,128]{3,1,2,0:T(8,128)(2,1)} %bitcast.69) | data formatting | bytes 16777216
  338.6 5.8 %fusion.34 = (bf16[1024,1024]{1,0:T(8,128)(2,1)S(1)}, bf16[1024,1024]{1,0:T(8,128)(2,1)}, bf16[1024,1024]{1,0:T(8,128)(2,1)}, bf16[1024,1024]{1,0:T(8,128)(2,1)}) fusion(bf16[1024,4096]{1,0:T(8,128)(2,1)} %param.6), kind=kLoop, calls=%fused_computation.57 | loop fusion | bytes 16777216 | tf_op jit(solution)/shard_map/slice | solution.py:76
  344.4 3.9 copy.37
  348.3 4.0 copy.38
  352.2 3.9 copy.39
  356.2 2.5 copy.40
  358.7 7.6 %convert_reduce_fusion = f32[1024]{0:T(1024)S(1)} fusion(bf16[1024,4,8,128]{3,2,1,0:T(8,128)(2,1)} %bitcast.70, s32[]{:T(128)S(6)} %select_n.36), kind=kLoop, calls=%fused_computation.32 | loop fusion | flops 1047552 | bytes 1052676 | tf_op jit(solution)/shard_map/reduce_sum | solution.py:62
  366.3 6.2 %select_reduce_fusion = f32[1024]{0:T(1024)S(1)} fusion(bf16[1024,4096]{1,0:T(8,128)(2,1)} %param.6, s32[1024]{0:T(1024)S(1)} %copy-done.6), kind=kLoop, calls=%fused_computation | loop fusion | flops 16776192 | bytes 8396800 | tf_op jit(solution)/shard_map/reduce_sum | solution.py:52
  372.5 20.5 %psum.7 = f32[2,1024]{1,0:T(2,128)S(1)} all-reduce(f32[2,1024]{1,0:T(2,128)S(1)} %pad_maximum_fusion), channel_id=1, replica_groups=mesh['loop'=16,'width'=8] {'width'}, use_global_device_ids=true, to_apply=%region_3.4 | all-reduce | flops 2048 | bytes 16384 | tf_op jit(solution)/shard_map/psum | solution.py:63
  393.1 5.4 %copy.35 = f32[8,1024,128]{1,2,0:T(8,128)} copy(f32[8,1024,128]{2,1,0:T(8,128)} %all-to-all-done.4) | data formatting | bytes 8388608 | tf_op jit(solution)/shard_map/all_to_all | solution.py:38
  398.4 5.4 %copy.32 = f32[8,1024,128]{1,2,0:T(8,128)} copy(f32[8,1024,128]{2,1,0:T(8,128)} %all-to-all-done.3) | data formatting | bytes 8388608 | tf_op jit(solution)/shard_map/all_to_all | solution.py:38
  403.8 5.4 %copy.29 = f32[8,1024,128]{1,2,0:T(8,128)} copy(f32[8,1024,128]{2,1,0:T(8,128)} %all-to-all-done.2) | data formatting | bytes 8388608 | tf_op jit(solution)/shard_map/all_to_all | solution.py:38
  409.2 5.1 broadcast_multiply_fusion
  414.3 2.6 broadcast_multiply_fusion.1
  416.9 1.1 copy-done.2
  418.0 2.4 broadcast_multiply_fusion.2
  420.4 5.4 copy.26
  425.8 5.2 broadcast_multiply_fusion.3
  431.0 0.8 copy-done.4
  431.8 8.4 %fusion.10 = (f32[1024,1024]{0,1:T(8,128)S(1)}, f32[1024,1024]{0,1:T(8,128)S(1)}, f32[1024,1024]{0,1:T(8,128)S(1)}, f32[1024,1024]{0,1:T(8,128)S(1)}) fusion(f32[8,1024,128]{1,2,0:T(8,128)S(1)} %copy-done.3, bf16[1024,1024]{0,1:T(8,128)(2,1)} %copy.40, f32[1024]{0:T(1024)S(1)} %select_reduce_fusion, f32[1024]{0:T(1024)S(1)} %bitcast.76, ...), kind=kLoop, calls=%fused_computation.13 | loop fusion | flops 33554432 | bytes 41971712 | tf_op jit(solution)/shard_map/mul | solution.py:79
  440.3 0.0 copy-start.5
  440.3 2.4 fusion.40
  442.7 0.1 collective-permute-start.6
  442.7 0.5 collective-permute-start.3
  443.2 23.0 %collective-permute-done.6 = f32[1024,512]{1,0:T(8,128)S(1)} collective-permute-done((f32[1024,512]{1,0:T(8,128)S(1)}, f32[1024,512]{1,0:T(8,128)S(1)}, u32[]{:S(2)}, u32[]{:S(2)}) %collective-permute-start.6) | collective-permute-done | bytes 2097184 | tf_op jit(solution)/shard_map/ppermute | solution.py:13
  466.3 2.4 convolution_add_fusion
  468.7 5.6 %collective-permute-start.7 = (f32[1024,512]{1,0:T(8,128)S(1)}, f32[1024,512]{1,0:T(8,128)S(1)}, u32[]{:S(2)}, u32[]{:S(2)}) collective-permute-start(f32[1024,512]{1,0:T(8,128)S(1)} %convolution_add_fusion), channel_id=1, source_target_pairs={{8,0},{16,8},{24,16},{32,24},{40,32},{48,40},{56,48},{64,56},{72,6... | collective-permute-start | bytes 6291464 | tf_op jit(solution)/shard_map/ppermute | solution.py:13
  474.2 17.8 %collective-permute-done.4 = bf16[1024,512]{1,0:T(8,128)(2,1)S(1)} collective-permute-done((bf16[1024,512]{1,0:T(8,128)(2,1)S(1)}, bf16[1024,512]{1,0:T(8,128)(2,1)S(1)}, u32[]{:S(2)}, u32[]{:S(2)}) %collective-permute-start.4) | collective-permute-done | bytes 1048608 | tf_op jit(solution)/shard_map/ppermute | solution.py:13
  492.1 2.4 fusion.41
  494.4 3.3 collective-permute-done.7
  497.8 0.5 add.95
  498.3 5.8 %collective-permute-start.8 = (f32[1024,512]{1,0:T(8,128)S(1)}, f32[1024,512]{1,0:T(8,128)S(1)}, u32[]{:S(2)}, u32[]{:S(2)}) collective-permute-start(f32[1024,512]{1,0:T(8,128)S(1)} %add.95), channel_id=1, source_target_pairs={{8,0},{16,8},{24,16},{32,24},{40,32},{48,40},{56,48},{64,56},{72,6... | collective-permute-start | bytes 6291464 | tf_op jit(solution)/shard_map/ppermute | solution.py:13
  504.1 2.3 fusion.42
  506.4 2.4 fusion.37
  508.8 2.4 fusion.39
  511.2 2.4 fusion.38
  513.6 3.8 add_add_fusion
  517.4 10.3 %collective-permute-done.8 = f32[1024,512]{1,0:T(8,128)S(1)} collective-permute-done((f32[1024,512]{1,0:T(8,128)S(1)}, f32[1024,512]{1,0:T(8,128)S(1)}, u32[]{:S(2)}, u32[]{:S(2)}) %collective-permute-start.8) | collective-permute-done | bytes 2097184 | tf_op jit(solution)/shard_map/ppermute | solution.py:13
  527.6 1.8 add.96
  (26 shorter events, 0.1 us)
Async XLA Ops:
  7.2 136.8 %copy-start.6 = (s32[1024]{0:T(1024)S(1)}, s32[1024]{0:T(1024)}, u32[]{:S(2)}) copy-start(s32[1024]{0:T(1024)} %param.7) | copy-start | bytes 12292
  7.2 136.8 %all-gather.2.cloned.1.call-start = ((), (), s32[]{:S(2)}) async-start(), calls=%async_computation.5 | async-start | bytes 9437184 | tf_op jit(solution)/shard_map/all_gather | solution.py:26
  34.6 40.5 %collective-permute-start = (bf16[128,4096]{0,1:T(8,128)(2,1)S(1)}, bf16[128,4096]{0,1:T(8,128)(2,1)S(1)}, u32[]{:S(2)}, u32[]{:S(2)}) collective-permute-start(bf16[128,4096]{0,1:T(8,128)(2,1)S(1)} %bitcast.73), channel_id=1, source_target_pairs={{120,0},{0,8},{8,16},{16,24},{24,32},{32,40},{40,48},{48,56},{56,6... | collective-permute-start | bytes 3145736 | tf_op jit(solution)/shard_map/ppermute | solution.py:13
  75.1 40.5 %collective-permute-start.1 = (bf16[128,4096]{0,1:T(8,128)(2,1)S(1)}, bf16[128,4096]{0,1:T(8,128)(2,1)}, u32[]{:S(2)}, u32[]{:S(2)}) collective-permute-start(bf16[128,4096]{0,1:T(8,128)(2,1)S(1)} %collective-permute-done), channel_id=1, source_target_pairs={{120,0},{0,8},{8,16},{16,24},{24,32},{32,40},{40,48},{48,56},{56,6... | collective-permute-start | bytes 3145736 | tf_op jit(solution)/shard_map/ppermute | solution.py:13
  115.7 28.3 %collective-permute-start.2 = (bf16[128,4096]{0,1:T(8,128)(2,1)}, bf16[128,4096]{0,1:T(8,128)(2,1)}, u32[]{:S(2)}, u32[]{:S(2)}) collective-permute-start(bf16[128,4096]{0,1:T(8,128)(2,1)} %collective-permute-done.1), channel_id=1, source_target_pairs={{120,0},{0,8},{8,16},{16,24},{24,32},{32,40},{40,48},{48,56},{56,6... | collective-permute-start | bytes 3145736 | tf_op jit(solution)/shard_map/ppermute | solution.py:13
  155.3 54.3 %all-to-all-start.4 = ((f32[8,1024,128]{2,1,0:T(8,128)}), f32[8,1024,128]{2,1,0:T(8,128)}, u32[]{:S(2)}, u32[]{:S(2)}) async-start(f32[8,1024,128]{2,1,0:T(8,128)} %stack.17), calls=%async_computation.4 | async-start | bytes 8388608 | tf_op jit(solution)/shard_map/all_to_all | solution.py:38
  211.8 54.1 %all-to-all-start.3 = ((f32[8,1024,128]{2,1,0:T(8,128)}), f32[8,1024,128]{2,1,0:T(8,128)}, u32[]{:S(2)}, u32[]{:S(2)}) async-start(f32[8,1024,128]{2,1,0:T(8,128)} %stack.16), calls=%async_computation.3 | async-start | bytes 8388608 | tf_op jit(solution)/shard_map/all_to_all | solution.py:38
  268.1 53.7 %all-to-all-start.2 = ((f32[8,1024,128]{2,1,0:T(8,128)}), f32[8,1024,128]{2,1,0:T(8,128)}, u32[]{:S(2)}, u32[]{:S(2)}) async-start(f32[8,1024,128]{2,1,0:T(8,128)} %stack.15), calls=%async_computation.2 | async-start | bytes 8388608 | tf_op jit(solution)/shard_map/all_to_all | solution.py:38
  324.1 96.4 %all-to-all-start.1 = ((f32[8,1024,128]{2,1,0:T(8,128)}), f32[8,1024,128]{2,1,0:T(8,128)}, u32[]{:S(2)}, u32[]{:S(2)}) async-start(f32[8,1024,128]{2,1,0:T(8,128)} %stack.14), calls=%async_computation.1 | async-start | bytes 8388608 | tf_op jit(solution)/shard_map/all_to_all | solution.py:38
  409.2 5.1 copy-start.1
  414.3 3.7 copy-start.2
  425.8 5.2 copy-start.3
  425.8 6.0 %copy-start.4 = (f32[8,1024,128]{1,2,0:T(8,128)S(1)}, f32[8,1024,128]{1,2,0:T(8,128)}, u32[]{:S(2)}) copy-start(f32[8,1024,128]{1,2,0:T(8,128)} %broadcast_multiply_fusion.1) | copy-start | bytes 12582916
  431.8 8.5 %copy-start = (bf16[1024,512]{1,0:T(8,128)(2,1)S(1)}, bf16[1024,512]{1,0:T(8,128)(2,1)}, u32[]{:S(2)}) copy-start(bf16[1024,512]{1,0:T(8,128)(2,1)} %param.4) | copy-start | bytes 3145732
  440.3 2.5 copy-start.5
  442.7 23.6 %collective-permute-start.6 = (f32[1024,512]{1,0:T(8,128)S(1)}, f32[1024,512]{1,0:T(8,128)S(1)}, u32[]{:S(2)}, u32[]{:S(2)}) collective-permute-start(f32[1024,512]{1,0:T(8,128)S(1)} %fusion.40), channel_id=1, source_target_pairs={{8,0},{16,8},{24,16},{32,24},{40,32},{48,40},{56,48},{64,56},{72,6... | collective-permute-start | bytes 6291464 | tf_op jit(solution)/shard_map/ppermute | solution.py:13
  442.7 31.5 %collective-permute-start.3 = (bf16[1024,512]{1,0:T(8,128)(2,1)S(1)}, bf16[1024,512]{1,0:T(8,128)(2,1)S(1)}, u32[]{:S(2)}, u32[]{:S(2)}) collective-permute-start(bf16[1024,512]{1,0:T(8,128)(2,1)S(1)} %copy-done.5), channel_id=1, source_target_pairs={{120,0},{0,8},{8,16},{16,24},{24,32},{32,40},{40,48},{48,56},{56,6... | collective-permute-start | bytes 3145736 | tf_op jit(solution)/shard_map/ppermute | solution.py:13
  468.7 29.1 %collective-permute-start.7 = (f32[1024,512]{1,0:T(8,128)S(1)}, f32[1024,512]{1,0:T(8,128)S(1)}, u32[]{:S(2)}, u32[]{:S(2)}) collective-permute-start(f32[1024,512]{1,0:T(8,128)S(1)} %convolution_add_fusion), channel_id=1, source_target_pairs={{8,0},{16,8},{24,16},{32,24},{40,32},{48,40},{56,48},{64,56},{72,6... | collective-permute-start | bytes 6291464 | tf_op jit(solution)/shard_map/ppermute | solution.py:13
  474.2 17.8 %collective-permute-start.4 = (bf16[1024,512]{1,0:T(8,128)(2,1)S(1)}, bf16[1024,512]{1,0:T(8,128)(2,1)S(1)}, u32[]{:S(2)}, u32[]{:S(2)}) collective-permute-start(bf16[1024,512]{1,0:T(8,128)(2,1)S(1)} %collective-permute-done.3), channel_id=1, source_target_pairs={{120,0},{0,8},{8,16},{16,24},{24,32},{32,40},{40,48},{48,56},{56,6... | collective-permute-start | bytes 3145736 | tf_op jit(solution)/shard_map/ppermute | solution.py:13
  492.1 21.5 %collective-permute-start.5 = (bf16[1024,512]{1,0:T(8,128)(2,1)S(1)}, bf16[1024,512]{1,0:T(8,128)(2,1)S(1)}, u32[]{:S(2)}, u32[]{:S(2)}) collective-permute-start(bf16[1024,512]{1,0:T(8,128)(2,1)S(1)} %collective-permute-done.4), channel_id=1, source_target_pairs={{120,0},{0,8},{8,16},{16,24},{24,32},{32,40},{40,48},{48,56},{56,6... | collective-permute-start | bytes 3145736 | tf_op jit(solution)/shard_map/ppermute | solution.py:13
  498.3 29.4 %collective-permute-start.8 = (f32[1024,512]{1,0:T(8,128)S(1)}, f32[1024,512]{1,0:T(8,128)S(1)}, u32[]{:S(2)}, u32[]{:S(2)}) collective-permute-start(f32[1024,512]{1,0:T(8,128)S(1)} %add.95), channel_id=1, source_target_pairs={{8,0},{16,8},{24,16},{32,24},{40,32},{48,40},{56,48},{64,56},{72,6... | collective-permute-start | bytes 6291464 | tf_op jit(solution)/shard_map/ppermute | solution.py:13
Sparse Core Ops, SparseCore 0:
  9.6 98.7 all-gather.1
